TPU v7x, 256 devices: a whole 4x4x8 slice. The times are simulated.
256 devices in a mesh: gx: 32 (over z_hi, y, x), gy: 2 (over core), gz: 4 (over z_lo).
Axes of the slice: x: 4, y: 4, z: 8 (z_hi: 2, z_lo: 4; z = z_hi * 4 + z_lo), core: 2. Of those that a mesh axis runs over, the one named last changes fastest.
Arguments:
- inputs: bfloat16 [4, 256, 32, 256], P(None, 'gx', 'gz', 'gy'), may hold values from -6 to 6
- w_in: bfloat16 [16, 4, 3, 3, 3], replicated, may hold values from -0.875 to 0.875
- w_fine_enc: bfloat16 [16, 16, 3, 3, 3], replicated, may hold values from -0.4375 to 0.4375
- w_down_mid: bfloat16 [64, 16, 2, 2, 2], replicated, may hold values from -0.75 to 0.75
- w_mid_enc: bfloat16 [27, 4096], replicated, may hold values from -0.21875 to 0.21875
- w_down_bottom: bfloat16 [8, 16384], replicated, may hold values from -0.375 to 0.375
- w_query: bfloat16 [256, 256], replicated, may hold values from -8 to 8
- w_key: bfloat16 [256, 256], replicated, may hold values from -0.375 to 0.375
- w_value: bfloat16 [256, 256], replicated, may hold values from -0.375 to 0.375
- w_attn_out: bfloat16 [256, 256], replicated, may hold values from -0.375 to 0.375
- w_up_mid: bfloat16 [8, 16384], replicated, may hold values from -0.375 to 0.375
- w_mid_dec: bfloat16 [27, 4096], replicated, may hold values from -0.21875 to 0.21875
- w_up_fine: bfloat16 [64, 16, 2, 2, 2], replicated, may hold values from -0.75 to 0.75
- w_fine_dec: bfloat16 [16, 16, 3, 3, 3], replicated, may hold values from -0.4375 to 0.4375
- w_head: bfloat16 [4, 16], replicated, may hold values from -1.5 to 1.5
Outputs:
- wake: float32 [4, 256, 32, 256], P(None, 'gx', 'gz', 'gy')
All inputs are finite; a program needn't handle non-finite values.
Results may differ from a plain program's by a relative error of at most 0.023.
The roundings to bfloat16 on the way count: a program that leaves them out, or rounds other values in their place, can miss the bound.
Values may be sent and summed in bfloat16 or wider, within the bound.
No kernel may reach another device: no remote copies, remote signals or barrier semaphores. Data moves between devices by JAX's collectives and lax.ppermute only.
A program may use at most 64 MiB of HBM per device.

v0:
```python
import jax
import jax.numpy as jnp
from jax import lax
from jax.experimental import pallas as pl
from jax.experimental.pallas import tpu as pltpu
from jax.sharding import PartitionSpec as P

C1 = 64
C2 = 256
HEADS = 4


NUMS = ("NCDHW", "OIDHW", "NCDHW")
FINE_SIDES = (("gx", 0), ("gy", 3), ("gz", 2))
MID_SIDES = (("gx", 1), ("gy", 3), ("gz", 2))


def extended(block, sides, width):
    for axis, dim in sides:
        count = lax.axis_size(axis)
        forward = [(i, i + 1) for i in range(count - 1)]
        backward = [(target, source) for source, target in forward]
        low = lax.ppermute(
            lax.slice_in_dim(block, block.shape[dim] - width, None, axis=dim), axis, forward
        )
        high = lax.ppermute(lax.slice_in_dim(block, 0, width, axis=dim), axis, backward)
        block = jnp.concatenate([low, block, high], axis=dim)
    return block


def unfold(weight, side, first, second):
    return weight.reshape(side, side, side, first, second).transpose(3, 4, 0, 1, 2)


def round_up(value, step):
    return (value + step - 1) // step * step


def band_weights(weight, sv, rows):
    out_c, in_c = weight.shape[:2]
    taps = jnp.arange(3)[:, None, None]
    eye = (jnp.arange(rows)[None, None, :] == jnp.arange(sv)[None, :, None] + taps).astype(
        jnp.float32
    )
    band = jnp.einsum("oiabc,bvw->acoviw", weight.astype(jnp.float32), eye)
    return band.reshape(9, out_c * sv, in_c * rows).astype(jnp.bfloat16)


def fine_kernel(p_ref, w_ref, *rest, sx, sv, ss, cout, head):
    if head:
        h_ref, o_ref = rest
    else:
        (o_ref,) = rest
    lanes = p_ref.shape[-1]
    for x in range(sx):
        acc = jnp.zeros((cout * sv, ss), jnp.float32)
        for a in range(3):
            slab = p_ref[x + a].astype(jnp.float32)
            for c in range(3):
                piece = slab if c == 0 else pltpu.roll(slab, lanes - c, 1)
                piece = piece[:, :ss].astype(jnp.bfloat16)
                acc = acc + jnp.dot(w_ref[a * 3 + c], piece, preferred_element_type=jnp.float32)
        act = (acc * jax.nn.sigmoid(acc)).astype(jnp.bfloat16)
        if head:
            res = jnp.dot(h_ref[...], act, preferred_element_type=jnp.float32)
            o_ref[:, x] = res.reshape(res.shape[0] // sv, sv, ss)
        else:
            o_ref[x] = act.astype(jnp.float32).reshape(cout, sv, ss)


def fine_conv(field, weight, head=None):
    sx, cin, sv, ss = field.shape
    cout = weight.shape[0]
    rows = round_up(sv + 2, 16)
    lanes = round_up(ss + 2, 128)
    padded = extended(field, FINE_SIDES, 1)
    padded = jnp.pad(padded, ((0, 0), (0, 0), (0, rows - sv - 2), (0, lanes - ss - 2)))
    padded = padded.reshape(sx + 2, cin * rows, lanes)
    operands = [padded, band_weights(weight, sv, rows)]
    if head is None:
        out_shape = jax.ShapeDtypeStruct((sx, cout, sv, ss), jnp.float32)
    else:
        eye = jnp.eye(sv, dtype=jnp.float32)
        kron = jnp.einsum("po,vw->pvow", head.astype(jnp.float32), eye)
        operands.append(kron.reshape(head.shape[0] * sv, cout * sv).astype(jnp.bfloat16))
        out_shape = jax.ShapeDtypeStruct((head.shape[0], sx, sv, ss), jnp.float32)
    kernel = lambda *refs: fine_kernel(
        *refs, sx=sx, sv=sv, ss=ss, cout=cout, head=head is not None
    )
    return pl.pallas_call(kernel, out_shape=out_shape)(*operands)


def conv_valid(padded, weight):
    return lax.conv_general_dilated(
        padded[None],
        weight,
        (1, 1, 1),
        "VALID",
        dimension_numbers=NUMS,
        preferred_element_type=jnp.float32,
    )[0]


def mid_conv(field, weight):
    padded = extended(field, MID_SIDES, 1)
    return conv_valid(padded, weight)


def conv_down(field, weight):
    return lax.conv_general_dilated(
        field[None],
        weight,
        (2, 2, 2),
        "VALID",
        dimension_numbers=NUMS,
        preferred_element_type=jnp.float32,
    )[0]


def fine_down(field, weight):
    sx, c, sv, ss = field.shape
    blocks = field.reshape(sx // 2, 2, c, sv // 2, 2, ss // 2, 2)
    return jnp.einsum("xaivbsc,oiabc->oxvs", blocks, weight, preferred_element_type=jnp.float32)


def fine_up(field, weight):
    outer = jnp.einsum("ixvs,ioabc->xaovbsc", field, weight, preferred_element_type=jnp.float32)
    chans, sx, sv, ss = (weight.shape[1], field.shape[1], field.shape[2], field.shape[3])
    return outer.reshape(2 * sx, chans, 2 * sv, 2 * ss)


def conv_up(field, weight):
    outer = jnp.einsum("ixvs,ioabc->oxavbsc", field, weight, preferred_element_type=jnp.float32)
    chans, sx, sv, ss = (weight.shape[1], field.shape[1], field.shape[2], field.shape[3])
    return outer.reshape(chans, 2 * sx, 2 * sv, 2 * ss)


def activate(value):
    return jax.nn.silu(value).astype(jnp.bfloat16)


def project(weight, field):
    return jnp.einsum("oc,cxp->oxp", weight, field, preferred_element_type=jnp.float32)


def normalize(block):
    values_f = block.astype(jnp.float32)
    mean_sq = jnp.mean(values_f * values_f, axis=0)
    return (values_f * lax.rsqrt(mean_sq + 1e-05)).astype(jnp.bfloat16)


def split_heads(weight, normed):
    chans, sx, count = normed.shape
    return project(weight, normed).astype(jnp.bfloat16).reshape(HEADS, chans // HEADS, sx, count)


def combine(queries, keys, values):
    scale = 1.0 / jnp.sqrt(jnp.float32(queries.shape[1]))
    scores = (
        jnp.einsum("hdxp,hdyp->hxyp", queries, keys, preferred_element_type=jnp.float32) * scale
    )
    weights = jax.nn.softmax(scores, axis=2).astype(jnp.bfloat16)
    attended = jnp.einsum("hxyp,hdyp->hdxp", weights, values, preferred_element_type=jnp.float32)
    heads, depth, sx, count = attended.shape
    return attended.astype(jnp.bfloat16).reshape(heads * depth, sx, count)


def finish(block, attended, w_attn_out):
    return (block.astype(jnp.float32) + project(w_attn_out, attended)).astype(jnp.bfloat16)


def on_device(
    inputs,
    w_in,
    w_fine_enc,
    w_down_mid,
    w_mid_enc,
    w_down_bottom,
    w_query,
    w_key,
    w_value,
    w_attn_out,
    w_up_mid,
    w_mid_dec,
    w_up_fine,
    w_fine_dec,
    w_head,
):
    fields = inputs.transpose(1, 0, 2, 3)
    first = fine_conv(fields, w_in).astype(jnp.bfloat16)
    fine_skip = fine_conv(first, w_fine_enc).astype(jnp.bfloat16)
    mid_in = activate(fine_down(fine_skip, w_down_mid))
    mid_skip = activate(mid_conv(mid_in, unfold(w_mid_enc, 3, C1, C1)))
    bottom = activate(conv_down(mid_skip, unfold(w_down_bottom, 2, C2, C1)))
    chans, sx, sv, ss = bottom.shape
    flat = bottom.reshape(chans, sx, sv * ss)
    rows = lax.all_to_all(flat, "gx", split_axis=2, concat_axis=1, tiled=True)
    normed = normalize(rows)
    queries = split_heads(w_query, normed)
    keys = split_heads(w_key, normed)
    values = split_heads(w_value, normed)
    result = finish(rows, combine(queries, keys, values), w_attn_out)
    mixed = lax.all_to_all(result, "gx", split_axis=1, concat_axis=2, tiled=True)
    bottom_out = mixed.reshape(chans, sx, sv, ss)
    mid_up = (
        conv_up(bottom_out, unfold(w_up_mid, 2, C2, C1)) + mid_skip.astype(jnp.float32)
    ).astype(jnp.bfloat16)
    mid_dec = activate(mid_conv(mid_up, unfold(w_mid_dec, 3, C1, C1)))
    fine_up_field = (fine_up(mid_dec, w_up_fine) + fine_skip.astype(jnp.float32)).astype(
        jnp.bfloat16
    )
    return fine_conv(fine_up_field, w_fine_dec, head=w_head)


def solution(mesh):
    placed = (P(None, "gx", "gz", "gy"),) + (P(),) * 14
    return jax.shard_map(
        on_device, mesh=mesh, in_specs=placed, out_specs=P(None, "gx", "gz", "gy"), check_vma=False
    )
```

profile of v0, /device:TPU:62, one launch (start us, length us, event | category | flops | bytes accessed | tf_op | source)
XLA Modules:
  0.0 284.9 jit_solution(9167497606391976466)
XLA Ops:
  0.8 7.8 %collective-permute-start = (bf16[1,4,8,128]{3,2,0,1:T(8,128)(2,1)S(1)}, bf16[1,4,8,128]{3,2,0,1:T(8,128)(2,1)S(1)}, u32[]{:S(2)}, u32[]{:S(2)}) collective-permute-start(bf16[1,4,8,128]{3,2,0,1:T(8,128)(2,1)S(1)} %get-tuple-element.33), channel_id=1, source_target_pairs={{0,8},{8,16},{16,24},{24,32},{32,40},{40,48},{48,56},{56,64},{64,7... | collective-permute-start | bytes 24584 | tf_op jit(solution)/shard_map/ppermute | solution.py:23
  10.5 11.7 %collective-permute-done.1 = bf16[1,4,8,128]{3,2,0,1:T(8,128)(2,1)S(1)} collective-permute-done((bf16[1,4,8,128]{3,2,0,1:T(8,128)(2,1)S(1)}, bf16[1,4,8,128]{3,2,0,1:T(8,128)(2,1)S(1)}, u32[]{:S(2)}, u32[]{:S(2)}) %collective-permute-start.1) | collective-permute-done | bytes 8224 | tf_op jit(solution)/shard_map/ppermute | solution.py:26
  46.3 3.9 %collective-permute-start.7 = (bf16[1,16,8,128]{3,2,1,0:T(8,128)(2,1)S(1)}, bf16[1,16,8,128]{3,2,1,0:T(8,128)(2,1)S(1)}, u32[]{:S(2)}, u32[]{:S(2)}) collective-permute-start(bf16[1,16,8,128]{3,2,1,0:T(8,128)(2,1)S(1)} %get-tuple-element.28), channel_id=1, source_target_pairs={{8,0},{16,8},{24,16},{32,24},{40,32},{48,40},{56,48},{64,56},{72,6... | collective-permute-start | bytes 98312 | tf_op jit(solution)/shard_map/ppermute | solution.py:26
  50.3 10.0 %collective-permute-done.7 = bf16[1,16,8,128]{3,2,1,0:T(8,128)(2,1)S(1)} collective-permute-done((bf16[1,16,8,128]{3,2,1,0:T(8,128)(2,1)S(1)}, bf16[1,16,8,128]{3,2,1,0:T(8,128)(2,1)S(1)}, u32[]{:S(2)}, u32[]{:S(2)}) %collective-permute-start.7) | collective-permute-done | bytes 32800 | tf_op jit(solution)/shard_map/ppermute | solution.py:26
  76.0 6.7 %copy.169 = bf16[3,3,16,8,16,16]{5,4,3,2,1,0:T(8,128)(2,1)} copy(bf16[3,3,16,8,16,16]{4,5,1,0,2,3:T(8,128)(2,1)} %convert_bitcast_fusion.1) | data formatting | bytes 1179648 | tf_op jit(solution)/shard_map/convert_element_type | solution.py:46
  82.7 6.9 %convert_element_type.132.refs_1_ = bf16[9,128,256]{2,1,0:T(8,128)(2,1)} reshape(bf16[3,3,16,8,16,16]{5,4,3,2,1,0:T(8,128)(2,1)} %copy.169) | data formatting | bytes 1179648 | tf_op jit(solution)/shard_map/convert_element_type | solution.py:46
  92.8 4.3 %shard_map.146 = f32[8,16,8,128]{3,2,1,0:T(8,128)} custom-call(bf16[10,256,256]{2,1,0:T(8,128)(2,1)} %bitcast.146, bf16[9,128,256]{2,1,0:T(8,128)(2,1)} %convert_element_type.132.refs_1_), custom_call_target="tpu_custom_call" | custom-call | tf_op jit(solution)/shard_map/pallas_call | solution.py:90
  101.9 3.9 %collective-permute-start.13 = (bf16[64,1,4,64]{0,3,2,1:T(8,128)(2,1)S(1)}, bf16[64,1,4,64]{0,3,2,1:T(8,128)(2,1)S(1)}, u32[]{:S(2)}, u32[]{:S(2)}) collective-permute-start(bf16[64,1,4,64]{0,3,2,1:T(8,128)(2,1)S(1)} %get-tuple-element.26), channel_id=1, source_target_pairs={{8,0},{16,8},{24,16},{32,24},{40,32},{48,40},{56,48},{64,56},{72,6... | collective-permute-start | bytes 98312 | tf_op jit(solution)/shard_map/ppermute | solution.py:26
  106.2 10.2 %collective-permute-done.13 = bf16[64,1,4,64]{0,3,2,1:T(8,128)(2,1)S(1)} collective-permute-done((bf16[64,1,4,64]{0,3,2,1:T(8,128)(2,1)S(1)}, bf16[64,1,4,64]{0,3,2,1:T(8,128)(2,1)S(1)}, u32[]{:S(2)}, u32[]{:S(2)}) %collective-permute-start.13) | collective-permute-done | bytes 32800 | tf_op jit(solution)/shard_map/ppermute | solution.py:26
  131.1 11.9 %fusion.50 = f32[1,64,4,4,64]{1,0,4,3,2:T(1,128)S(1)} fusion(bf16[3,3,3,64,64]{4,3,2,1,0:T(8,128)(2,1)S(1)} %reshape.97, bf16[1,64,6,6,66]{1,4,3,2,0:T(8,128)(2,1)S(1)} %maximum_bitcast_fusion), kind=kOutput, calls=%fused_computation.55 | convolution fusion | flops 226492416 | bytes 787456 | tf_op jit(solution)/shard_map/conv_general_dilated | solution.py:94
  144.3 15.7 %all_to_all.24 = bf16[256,2,64]{0,1,2:T(2,128)(2,1)S(1)} all-to-all(bf16[256,2,64]{0,1,2:T(2,128)(2,1)S(1)} %copy.181), channel_id=1, replica_groups=mesh['gx'=32,'gy'=2,'gz'=4] {'gx'}, dimensions={2} | all-to-all | bytes 131072 | tf_op jit(solution)/shard_map/all_to_all | solution.py:197
  163.6 6.9 %all-to-all-start.1 = ((bf16[256,64,2]{0,2,1:T(2,128)(2,1)}), bf16[256,64,2]{0,2,1:T(2,128)(2,1)S(1)}, u32[]{:S(2)}, u32[]{:S(2)}) async-start(bf16[256,64,2]{0,2,1:T(2,128)(2,1)} %copy.190), calls=%async_computation.1 | async-start | bytes 131072 | tf_op jit(solution)/shard_map/all_to_all | solution.py:203
  171.1 8.6 %all-to-all-done.1 = bf16[256,64,2]{0,2,1:T(2,128)(2,1)S(1)} async-done(((bf16[256,64,2]{0,2,1:T(2,128)(2,1)}), bf16[256,64,2]{0,2,1:T(2,128)(2,1)S(1)}, u32[]{:S(2)}, u32[]{:S(2)}) %all-to-all-start.1) | async-done | bytes 65568 | tf_op jit(solution)/shard_map/all_to_all | solution.py:203
  180.6 5.3 %collective-permute-start.18 = (bf16[64,1,4,64]{0,3,2,1:T(8,128)(2,1)S(1)}, bf16[64,1,4,64]{0,3,2,1:T(8,128)(2,1)S(1)}, u32[]{:S(2)}, u32[]{:S(2)}) collective-permute-start(bf16[64,1,4,64]{0,3,2,1:T(8,128)(2,1)S(1)} %get-tuple-element.23), channel_id=1, source_target_pairs={{0,8},{8,16},{16,24},{24,32},{32,40},{40,48},{48,56},{56,64},{64,7... | collective-permute-start | bytes 98312 | tf_op jit(solution)/shard_map/ppermute | solution.py:23
  187.8 12.3 %collective-permute-done.19 = bf16[64,1,4,64]{0,3,2,1:T(8,128)(2,1)S(1)} collective-permute-done((bf16[64,1,4,64]{0,3,2,1:T(8,128)(2,1)S(1)}, bf16[64,1,4,64]{0,3,2,1:T(8,128)(2,1)S(1)}, u32[]{:S(2)}, u32[]{:S(2)}) %collective-permute-start.19) | collective-permute-done | bytes 32800 | tf_op jit(solution)/shard_map/ppermute | solution.py:26
  207.1 3.6 %collective-permute-start.23 = (bf16[64,6,1,66]{0,3,2,1:T(8,128)(2,1)S(1)}, bf16[64,6,1,66]{0,3,2,1:T(8,128)(2,1)S(1)}, u32[]{:S(2)}, u32[]{:S(2)}) collective-permute-start(bf16[64,6,1,66]{0,3,2,1:T(8,128)(2,1)S(1)} %get-tuple-element.10), channel_id=1, source_target_pairs={{1,0},{2,1},{3,2},{5,4},{6,5},{7,6},{9,8},{10,9},{11,10},{13,12},{... | collective-permute-start | bytes 152072 | tf_op jit(solution)/shard_map/ppermute | solution.py:26
  214.3 11.9 %fusion.48 = f32[1,64,4,4,64]{1,0,4,3,2:T(1,128)S(1)} fusion(bf16[3,3,3,64,64]{4,3,2,1,0:T(8,128)(2,1)S(1)} %reshape.106, bf16[1,64,6,6,66]{1,4,3,2,0:T(8,128)(2,1)S(1)} %maximum_bitcast_fusion.1), kind=kOutput, calls=%fused_computation.53 | convolution fusion | flops 226492416 | bytes 787456 | tf_op jit(solution)/shard_map/conv_general_dilated | solution.py:94
  226.7 4.4 %copy.197 = f32[4,2,16,4,2,64,2]{2,6,5,4,3,1,0:T(2,128)} copy(f32[4,2,16,4,2,64,2]{5,2,6,4,1,3,0:T(8,128)S(1)} %convolution_bitcast_fusion) | data formatting | bytes 1048576 | tf_op jit(solution)/shard_map/ixvs,ioabc->xaovbsc/transpose | solution.py:127
  235.9 3.9 %collective-permute-start.25 = (bf16[1,16,8,128]{3,2,1,0:T(8,128)(2,1)S(1)}, bf16[1,16,8,128]{3,2,1,0:T(8,128)(2,1)S(1)}, u32[]{:S(2)}, u32[]{:S(2)}) collective-permute-start(bf16[1,16,8,128]{3,2,1,0:T(8,128)(2,1)S(1)} %get-tuple-element.22), channel_id=1, source_target_pairs={{8,0},{16,8},{24,16},{32,24},{40,32},{48,40},{56,48},{64,56},{72,6... | collective-permute-start | bytes 98312 | tf_op jit(solution)/shard_map/ppermute | solution.py:26
  243.3 6.7 %collective-permute-done.25 = bf16[1,16,8,128]{3,2,1,0:T(8,128)(2,1)S(1)} collective-permute-done((bf16[1,16,8,128]{3,2,1,0:T(8,128)(2,1)S(1)}, bf16[1,16,8,128]{3,2,1,0:T(8,128)(2,1)S(1)}, u32[]{:S(2)}, u32[]{:S(2)}) %collective-permute-start.25) | collective-permute-done | bytes 32800 | tf_op jit(solution)/shard_map/ppermute | solution.py:26
  258.3 3.7 %collective-permute-start.29 = (bf16[10,16,1,130]{3,2,1,0:T(2,128)(2,1)S(1)}, bf16[10,16,1,130]{3,2,1,0:T(2,128)(2,1)S(1)}, u32[]{:S(2)}, u32[]{:S(2)}) collective-permute-start(bf16[10,16,1,130]{3,2,1,0:T(2,128)(2,1)S(1)} %get-tuple-element.6), channel_id=1, source_target_pairs={{1,0},{2,1},{3,2},{5,4},{6,5},{7,6},{9,8},{10,9},{11,10},{13,12},{... | collective-permute-start | bytes 124808 | tf_op jit(solution)/shard_map/ppermute | solution.py:26
  262.1 6.7 %copy.200 = bf16[3,3,16,8,16,16]{5,4,3,2,1,0:T(8,128)(2,1)} copy(bf16[3,3,16,8,16,16]{4,5,1,0,2,3:T(8,128)(2,1)} %convert_bitcast_fusion) | data formatting | bytes 1179648 | tf_op jit(solution)/shard_map/convert_element_type | solution.py:46
  268.8 6.9 %convert_element_type.161.refs_1_ = bf16[9,128,256]{2,1,0:T(8,128)(2,1)} reshape(bf16[3,3,16,8,16,16]{5,4,3,2,1,0:T(8,128)(2,1)} %copy.200) | data formatting | bytes 1179648 | tf_op jit(solution)/shard_map/convert_element_type | solution.py:46
  279.6 5.0 %shard_map.147 = f32[4,8,8,128]{3,2,1,0:T(8,128)} custom-call(bf16[10,256,256]{2,1,0:T(8,128)(2,1)} %bitcast.145, bf16[9,128,256]{2,1,0:T(8,128)(2,1)} %convert_element_type.161.refs_1_, bf16[32,128]{1,0:T(8,128)(2,1)} %convert_element_type.164.refs_2_), custom_call_target="tpu_custom_call" | custom-call | tf_op jit(solution)/shard_map/pallas_call | solution.py:90
  (161 shorter events, 104.5 us)
Async XLA Ops:
  0.8 9.7 %collective-permute-start = (bf16[1,4,8,128]{3,2,0,1:T(8,128)(2,1)S(1)}, bf16[1,4,8,128]{3,2,0,1:T(8,128)(2,1)S(1)}, u32[]{:S(2)}, u32[]{:S(2)}) collective-permute-start(bf16[1,4,8,128]{3,2,0,1:T(8,128)(2,1)S(1)} %get-tuple-element.33), channel_id=1, source_target_pairs={{0,8},{8,16},{16,24},{24,32},{32,40},{40,48},{48,56},{56,64},{64,7... | collective-permute-start | bytes 24584 | tf_op jit(solution)/shard_map/ppermute | solution.py:23
  8.5 13.7 %collective-permute-start.1 = (bf16[1,4,8,128]{3,2,0,1:T(8,128)(2,1)S(1)}, bf16[1,4,8,128]{3,2,0,1:T(8,128)(2,1)S(1)}, u32[]{:S(2)}, u32[]{:S(2)}) collective-permute-start(bf16[1,4,8,128]{3,2,0,1:T(8,128)(2,1)S(1)} %get-tuple-element.34), channel_id=1, source_target_pairs={{8,0},{16,8},{24,16},{32,24},{40,32},{48,40},{56,48},{64,56},{72,6... | collective-permute-start | bytes 24584 | tf_op jit(solution)/shard_map/ppermute | solution.py:26
  24.4 3.2 %collective-permute-start.3 = (bf16[10,4,8,1]{3,2,0,1:T(8,128)(2,1)S(1)}, bf16[10,4,8,1]{3,2,0,1:T(8,128)(2,1)S(1)}, u32[]{:S(2)}, u32[]{:S(2)}) collective-permute-start(bf16[10,4,8,1]{3,2,0,1:T(8,128)(2,1)S(1)} %get-tuple-element.32), channel_id=1, source_target_pairs={{4,0},{5,1},{6,2},{7,3},{12,8},{13,9},{14,10},{15,11},{20,16},{21,... | collective-permute-start | bytes 1928 | tf_op jit(solution)/shard_map/ppermute | solution.py:26
  28.8 10.6 %collective-permute-start.4 = (bf16[10,4,1,130]{3,2,0,1:T(2,128)(2,1)S(1)}, bf16[10,4,1,130]{3,2,0,1:T(2,128)(2,1)S(1)}, u32[]{:S(2)}, u32[]{:S(2)}) collective-permute-start(bf16[10,4,1,130]{3,2,0,1:T(2,128)(2,1)S(1)} %get-tuple-element.29), channel_id=1, source_target_pairs={{0,1},{1,2},{2,3},{4,5},{5,6},{6,7},{8,9},{9,10},{10,11},{12,13},{... | collective-permute-start | bytes 31208 | tf_op jit(solution)/shard_map/ppermute | solution.py:23
  31.8 7.6 %collective-permute-start.5 = (bf16[10,4,1,130]{3,2,0,1:T(2,128)(2,1)S(1)}, bf16[10,4,1,130]{3,2,0,1:T(2,128)(2,1)S(1)}, u32[]{:S(2)}, u32[]{:S(2)}) collective-permute-start(bf16[10,4,1,130]{3,2,0,1:T(2,128)(2,1)S(1)} %get-tuple-element.30), channel_id=1, source_target_pairs={{1,0},{2,1},{3,2},{5,4},{6,5},{7,6},{9,8},{10,9},{11,10},{13,12},{... | collective-permute-start | bytes 31208 | tf_op jit(solution)/shard_map/ppermute | solution.py:26
  44.4 5.9 %collective-permute-start.6 = (bf16[1,16,8,128]{3,2,1,0:T(8,128)(2,1)S(1)}, bf16[1,16,8,128]{3,2,1,0:T(8,128)(2,1)S(1)}, u32[]{:S(2)}, u32[]{:S(2)}) collective-permute-start(bf16[1,16,8,128]{3,2,1,0:T(8,128)(2,1)S(1)} %get-tuple-element.27), channel_id=1, source_target_pairs={{0,8},{8,16},{16,24},{24,32},{32,40},{40,48},{48,56},{56,64},{64,7... | collective-permute-start | bytes 98312 | tf_op jit(solution)/shard_map/ppermute | solution.py:23
  46.3 14.0 %collective-permute-start.7 = (bf16[1,16,8,128]{3,2,1,0:T(8,128)(2,1)S(1)}, bf16[1,16,8,128]{3,2,1,0:T(8,128)(2,1)S(1)}, u32[]{:S(2)}, u32[]{:S(2)}) collective-permute-start(bf16[1,16,8,128]{3,2,1,0:T(8,128)(2,1)S(1)} %get-tuple-element.28), channel_id=1, source_target_pairs={{8,0},{16,8},{24,16},{32,24},{40,32},{48,40},{56,48},{64,56},{72,6... | collective-permute-start | bytes 98312 | tf_op jit(solution)/shard_map/ppermute | solution.py:26
  61.9 3.5 %collective-permute-start.9 = (bf16[10,16,8,1]{3,2,1,0:T(8,128)(2,1)S(1)}, bf16[10,16,8,1]{3,2,1,0:T(8,128)(2,1)S(1)}, u32[]{:S(2)}, u32[]{:S(2)}) collective-permute-start(bf16[10,16,8,1]{3,2,1,0:T(8,128)(2,1)S(1)} %get-tuple-element.20), channel_id=1, source_target_pairs={{4,0},{5,1},{6,2},{7,3},{12,8},{13,9},{14,10},{15,11},{20,16},{21,... | collective-permute-start | bytes 7688 | tf_op jit(solution)/shard_map/ppermute | solution.py:26
  66.2 23.4 %collective-permute-start.10 = (bf16[10,16,1,130]{3,2,1,0:T(2,128)(2,1)S(1)}, bf16[10,16,1,130]{3,2,1,0:T(2,128)(2,1)S(1)}, u32[]{:S(2)}, u32[]{:S(2)}) collective-permute-start(bf16[10,16,1,130]{3,2,1,0:T(2,128)(2,1)S(1)} %get-tuple-element.7), channel_id=1, source_target_pairs={{0,1},{1,2},{2,3},{4,5},{5,6},{6,7},{8,9},{9,10},{10,11},{12,13},{... | collective-permute-start | bytes 124808 | tf_op jit(solution)/shard_map/ppermute | solution.py:23
  69.2 20.4 %collective-permute-start.11 = (bf16[10,16,1,130]{3,2,1,0:T(2,128)(2,1)S(1)}, bf16[10,16,1,130]{3,2,1,0:T(2,128)(2,1)S(1)}, u32[]{:S(2)}, u32[]{:S(2)}) collective-permute-start(bf16[10,16,1,130]{3,2,1,0:T(2,128)(2,1)S(1)} %get-tuple-element.8), channel_id=1, source_target_pairs={{1,0},{2,1},{3,2},{5,4},{6,5},{7,6},{9,8},{10,9},{11,10},{13,12},{... | collective-permute-start | bytes 124808 | tf_op jit(solution)/shard_map/ppermute | solution.py:26
  99.9 6.3 %collective-permute-start.12 = (bf16[64,1,4,64]{0,3,2,1:T(8,128)(2,1)S(1)}, bf16[64,1,4,64]{0,3,2,1:T(8,128)(2,1)S(1)}, u32[]{:S(2)}, u32[]{:S(2)}) collective-permute-start(bf16[64,1,4,64]{0,3,2,1:T(8,128)(2,1)S(1)} %get-tuple-element.25), channel_id=1, source_target_pairs={{0,8},{8,16},{16,24},{24,32},{32,40},{40,48},{48,56},{56,64},{64,7... | collective-permute-start | bytes 98312 | tf_op jit(solution)/shard_map/ppermute | solution.py:23
  101.9 14.5 %collective-permute-start.13 = (bf16[64,1,4,64]{0,3,2,1:T(8,128)(2,1)S(1)}, bf16[64,1,4,64]{0,3,2,1:T(8,128)(2,1)S(1)}, u32[]{:S(2)}, u32[]{:S(2)}) collective-permute-start(bf16[64,1,4,64]{0,3,2,1:T(8,128)(2,1)S(1)} %get-tuple-element.26), channel_id=1, source_target_pairs={{8,0},{16,8},{24,16},{32,24},{40,32},{48,40},{56,48},{64,56},{72,6... | collective-permute-start | bytes 98312 | tf_op jit(solution)/shard_map/ppermute | solution.py:26
  120.9 7.0 %collective-permute-start.16 = (bf16[64,6,1,66]{0,3,2,1:T(8,128)(2,1)S(1)}, bf16[64,6,1,66]{0,3,2,1:T(8,128)(2,1)S(1)}, u32[]{:S(2)}, u32[]{:S(2)}) collective-permute-start(bf16[64,6,1,66]{0,3,2,1:T(8,128)(2,1)S(1)} %get-tuple-element.11), channel_id=1, source_target_pairs={{0,1},{1,2},{2,3},{4,5},{5,6},{6,7},{8,9},{9,10},{10,11},{12,13},{... | collective-permute-start | bytes 152072 | tf_op jit(solution)/shard_map/ppermute | solution.py:23
  124.1 6.7 %collective-permute-start.17 = (bf16[64,6,1,66]{0,3,2,1:T(8,128)(2,1)S(1)}, bf16[64,6,1,66]{0,3,2,1:T(8,128)(2,1)S(1)}, u32[]{:S(2)}, u32[]{:S(2)}) collective-permute-start(bf16[64,6,1,66]{0,3,2,1:T(8,128)(2,1)S(1)} %get-tuple-element.12), channel_id=1, source_target_pairs={{1,0},{2,1},{3,2},{5,4},{6,5},{7,6},{9,8},{10,9},{11,10},{13,12},{... | collective-permute-start | bytes 152072 | tf_op jit(solution)/shard_map/ppermute | solution.py:26
  163.6 16.1 %all-to-all-start.1 = ((bf16[256,64,2]{0,2,1:T(2,128)(2,1)}), bf16[256,64,2]{0,2,1:T(2,128)(2,1)S(1)}, u32[]{:S(2)}, u32[]{:S(2)}) async-start(bf16[256,64,2]{0,2,1:T(2,128)(2,1)} %copy.190), calls=%async_computation.1 | async-start | bytes 131072 | tf_op jit(solution)/shard_map/all_to_all | solution.py:203
  180.6 7.2 %collective-permute-start.18 = (bf16[64,1,4,64]{0,3,2,1:T(8,128)(2,1)S(1)}, bf16[64,1,4,64]{0,3,2,1:T(8,128)(2,1)S(1)}, u32[]{:S(2)}, u32[]{:S(2)}) collective-permute-start(bf16[64,1,4,64]{0,3,2,1:T(8,128)(2,1)S(1)} %get-tuple-element.23), channel_id=1, source_target_pairs={{0,8},{8,16},{16,24},{24,32},{32,40},{40,48},{48,56},{56,64},{64,7... | collective-permute-start | bytes 98312 | tf_op jit(solution)/shard_map/ppermute | solution.py:23
  185.9 14.3 %collective-permute-start.19 = (bf16[64,1,4,64]{0,3,2,1:T(8,128)(2,1)S(1)}, bf16[64,1,4,64]{0,3,2,1:T(8,128)(2,1)S(1)}, u32[]{:S(2)}, u32[]{:S(2)}) collective-permute-start(bf16[64,1,4,64]{0,3,2,1:T(8,128)(2,1)S(1)} %get-tuple-element.24), channel_id=1, source_target_pairs={{8,0},{16,8},{24,16},{32,24},{40,32},{48,40},{56,48},{64,56},{72,6... | collective-permute-start | bytes 98312 | tf_op jit(solution)/shard_map/ppermute | solution.py:26
  204.7 7.0 %collective-permute-start.22 = (bf16[64,6,1,66]{0,3,2,1:T(8,128)(2,1)S(1)}, bf16[64,6,1,66]{0,3,2,1:T(8,128)(2,1)S(1)}, u32[]{:S(2)}, u32[]{:S(2)}) collective-permute-start(bf16[64,6,1,66]{0,3,2,1:T(8,128)(2,1)S(1)} %get-tuple-element.9), channel_id=1, source_target_pairs={{0,1},{1,2},{2,3},{4,5},{5,6},{6,7},{8,9},{9,10},{10,11},{12,13},{... | collective-permute-start | bytes 152072 | tf_op jit(solution)/shard_map/ppermute | solution.py:23
  207.1 7.0 %collective-permute-start.23 = (bf16[64,6,1,66]{0,3,2,1:T(8,128)(2,1)S(1)}, bf16[64,6,1,66]{0,3,2,1:T(8,128)(2,1)S(1)}, u32[]{:S(2)}, u32[]{:S(2)}) collective-permute-start(bf16[64,6,1,66]{0,3,2,1:T(8,128)(2,1)S(1)} %get-tuple-element.10), channel_id=1, source_target_pairs={{1,0},{2,1},{3,2},{5,4},{6,5},{7,6},{9,8},{10,9},{11,10},{13,12},{... | collective-permute-start | bytes 152072 | tf_op jit(solution)/shard_map/ppermute | solution.py:26
  234.0 9.3 %collective-permute-start.24 = (bf16[1,16,8,128]{3,2,1,0:T(8,128)(2,1)S(1)}, bf16[1,16,8,128]{3,2,1,0:T(8,128)(2,1)S(1)}, u32[]{:S(2)}, u32[]{:S(2)}) collective-permute-start(bf16[1,16,8,128]{3,2,1,0:T(8,128)(2,1)S(1)} %get-tuple-element.21), channel_id=1, source_target_pairs={{0,8},{8,16},{16,24},{24,32},{32,40},{40,48},{48,56},{56,64},{64,7... | collective-permute-start | bytes 98312 | tf_op jit(solution)/shard_map/ppermute | solution.py:23
  235.9 14.1 %collective-permute-start.25 = (bf16[1,16,8,128]{3,2,1,0:T(8,128)(2,1)S(1)}, bf16[1,16,8,128]{3,2,1,0:T(8,128)(2,1)S(1)}, u32[]{:S(2)}, u32[]{:S(2)}) collective-permute-start(bf16[1,16,8,128]{3,2,1,0:T(8,128)(2,1)S(1)} %get-tuple-element.22), channel_id=1, source_target_pairs={{8,0},{16,8},{24,16},{32,24},{40,32},{48,40},{56,48},{64,56},{72,6... | collective-permute-start | bytes 98312 | tf_op jit(solution)/shard_map/ppermute | solution.py:26
  251.5 3.5 %collective-permute-start.27 = (bf16[10,16,8,1]{3,2,1,0:T(8,128)(2,1)S(1)}, bf16[10,16,8,1]{3,2,1,0:T(8,128)(2,1)S(1)}, u32[]{:S(2)}, u32[]{:S(2)}) collective-permute-start(bf16[10,16,8,1]{3,2,1,0:T(8,128)(2,1)S(1)} %get-tuple-element.18), channel_id=1, source_target_pairs={{4,0},{5,1},{6,2},{7,3},{12,8},{13,9},{14,10},{15,11},{20,16},{21,... | collective-permute-start | bytes 7688 | tf_op jit(solution)/shard_map/ppermute | solution.py:26
  255.8 20.6 %collective-permute-start.28 = (bf16[10,16,1,130]{3,2,1,0:T(2,128)(2,1)S(1)}, bf16[10,16,1,130]{3,2,1,0:T(2,128)(2,1)S(1)}, u32[]{:S(2)}, u32[]{:S(2)}) collective-permute-start(bf16[10,16,1,130]{3,2,1,0:T(2,128)(2,1)S(1)} %get-tuple-element.5), channel_id=1, source_target_pairs={{0,1},{1,2},{2,3},{4,5},{5,6},{6,7},{8,9},{9,10},{10,11},{12,13},{... | collective-permute-start | bytes 124808 | tf_op jit(solution)/shard_map/ppermute | solution.py:23
  258.3 18.2 %collective-permute-start.29 = (bf16[10,16,1,130]{3,2,1,0:T(2,128)(2,1)S(1)}, bf16[10,16,1,130]{3,2,1,0:T(2,128)(2,1)S(1)}, u32[]{:S(2)}, u32[]{:S(2)}) collective-permute-start(bf16[10,16,1,130]{3,2,1,0:T(2,128)(2,1)S(1)} %get-tuple-element.6), channel_id=1, source_target_pairs={{1,0},{2,1},{3,2},{5,4},{6,5},{7,6},{9,8},{10,9},{11,10},{13,12},{... | collective-permute-start | bytes 124808 | tf_op jit(solution)/shard_map/ppermute | solution.py:26
  (22 other events, 340.0 us)
where the time goes:
time: 291 us; the launch traced here: 285 us
  starting transfers between devices  84.8 us (29%)
  waiting for transfers between devices  75.5 us (26%)
  local copies, waits for them, and re-layouts  46.5 us (16%)
  matrix products  34.9 us (12%)
  blocking collectives  15.7 us (5%)
  other arithmetic  14 us (5%)
  Pallas kernels  12.1 us (4%)
    ppermute x15, waiting for transfers between devices, extended(): lax.ppermute(lax.slice_in_dim(block, 0, width, axis=dim), axis, backward)  66.1 us
    ppermute x15, starting transfers between devices, extended(): lax.ppermute(lax.slice_in_dim(block, block.shape[dim] - width, None, axis...  39.5 us
    ppermute x15, starting transfers between devices, extended(): lax.ppermute(lax.slice_in_dim(block, 0, width, axis=dim), axis, backward)  38.4 us
    convert_element_type x6, local copies, waits for them, and re-layouts, band_weights(): return band.reshape(9, out_c * sv, in_c * rows).astype(jnp.bfloat16)  30.5 us
    conv_general_dilated x2, matrix products, conv_valid(): lax.conv_general_dilated(padded[None], weight, (1, 1, 1), 'VALID', dimens...  23.8 us
    all_to_all x1, blocking collectives, on_device(): rows = lax.all_to_all(flat, 'gx', split_axis=2, concat_axis=1, tiled=True)  15.7 us
    pallas_call x3, Pallas kernels, fine_conv(): return pl.pallas_call(kernel, out_shape=out_shape)(*operands)  12.1 us
    all_to_all x1, waiting for transfers between devices, on_device(): lax.all_to_all(result, 'gx', split_axis=1, concat_axis=2, tiled=True)  8.59 us
  transfers between devices with their start and end apart: 31, of which 15 were waited for; matrix products, arithmetic and copies ran while one was open for 15% of the time, Pallas kernels for 0%

commit v1 on v0

--- a/solution.py
+++ b/solution.py
@@ -38,11 +38,12 @@
 
 def band_weights(weight, sv, rows):
     out_c, in_c = weight.shape[:2]
-    taps = jnp.arange(3)[:, None, None]
-    eye = (jnp.arange(rows)[None, None, :] == jnp.arange(sv)[None, :, None] + taps).astype(
-        jnp.float32
-    )
-    band = jnp.einsum("oiabc,bvw->acoviw", weight.astype(jnp.float32), eye)
+    taps = weight.astype(jnp.float32).transpose(2, 4, 0, 3, 1)
+    shift = jnp.arange(rows)[None, :] - jnp.arange(sv)[:, None]
+    band = sum(
+        jnp.where((shift == b)[None, None, None, :, None, :], taps[:, :, :, b, None, :, None], 0.0)
+        for b in range(3)
+    )
     return band.reshape(9, out_c * sv, in_c * rows).astype(jnp.bfloat16)
 
 
@@ -189,7 +190,7 @@
     fields = inputs.transpose(1, 0, 2, 3)
     first = fine_conv(fields, w_in).astype(jnp.bfloat16)
     fine_skip = fine_conv(first, w_fine_enc).astype(jnp.bfloat16)
-    mid_in = activate(fine_down(fine_skip, w_down_mid))
+    mid_in = activate(conv_down(fine_skip.transpose(1, 0, 2, 3), w_down_mid))
     mid_skip = activate(mid_conv(mid_in, unfold(w_mid_enc, 3, C1, C1)))
     bottom = activate(conv_down(mid_skip, unfold(w_down_bottom, 2, C2, C1)))
     chans, sx, sv, ss = bottom.shape

time: 291 us -> 361 us (1.24)
  the two profiles are of different devices: /device:TPU:62 before, /device:TPU:30 now
where the time goes in v1:
time: 361 us; the launch traced here: 354 us
  local copies, waits for them, and re-layouts  108 us (30%)
  waiting for transfers between devices  86 us (24%)
  starting transfers between devices  82.4 us (23%)
  matrix products  29 us (8%)
  other arithmetic  19.1 us (5%)
  blocking collectives  15.7 us (4%)
  Pallas kernels  12.1 us (3%)
    broadcast_in_dim x36, local copies, waits for them, and re-layouts, band_weights(): jnp.where((shift == b)[None, None, None, :, None, :], taps[:, :, :, b, No...  85.8 us
    ppermute x15, waiting for transfers between devices, extended(): lax.ppermute(lax.slice_in_dim(block, 0, width, axis=dim), axis, backward)  74.8 us
    ppermute x15, starting transfers between devices, extended(): lax.ppermute(lax.slice_in_dim(block, block.shape[dim] - width, None, axis...  47.6 us
    ppermute x15, starting transfers between devices, extended(): lax.ppermute(lax.slice_in_dim(block, 0, width, axis=dim), axis, backward)  27.8 us
    conv_general_dilated x2, matrix products, conv_valid(): lax.conv_general_dilated(padded[None], weight, (1, 1, 1), 'VALID', dimens...  23.8 us
    all_to_all x1, blocking collectives, on_device(): rows = lax.all_to_all(flat, 'gx', split_axis=2, concat_axis=1, tiled=True)  15.7 us
    pallas_call x3, Pallas kernels, fine_conv(): return pl.pallas_call(kernel, out_shape=out_shape)(*operands)  12.1 us
    all_to_all x1, waiting for transfers between devices, on_device(): lax.all_to_all(result, 'gx', split_axis=1, concat_axis=2, tiled=True)  8.59 us
  transfers between devices with their start and end apart: 31, of which 20 were waited for; matrix products, arithmetic and copies ran while one was open for 27% of the time, Pallas kernels for 0%

profile of v1, /device:TPU:30, one launch (start us, length us, event | category | flops | bytes accessed | tf_op | source)
XLA Modules:
  0.0 353.6 jit_solution(7556573730429085618)
XLA Ops:
  0.8 8.7 %collective-permute-start = (bf16[1,4,8,128]{3,2,0,1:T(8,128)(2,1)S(1)}, bf16[1,4,8,128]{3,2,0,1:T(8,128)(2,1)S(1)}, u32[]{:S(2)}, u32[]{:S(2)}) collective-permute-start(bf16[1,4,8,128]{3,2,0,1:T(8,128)(2,1)S(1)} %get-tuple-element.41), channel_id=1, source_target_pairs={{0,8},{8,16},{16,24},{24,32},{32,40},{40,48},{48,56},{56,64},{64,7... | collective-permute-start | bytes 24584 | tf_op jit(solution)/shard_map/ppermute | solution.py:23
  41.7 10.0 %collective-permute-start.6 = (bf16[1,16,8,128]{3,2,1,0:T(8,128)(2,1)S(1)}, bf16[1,16,8,128]{3,2,1,0:T(8,128)(2,1)S(1)}, u32[]{:S(2)}, u32[]{:S(2)}) collective-permute-start(bf16[1,16,8,128]{3,2,1,0:T(8,128)(2,1)S(1)} %get-tuple-element.27), channel_id=1, source_target_pairs={{0,8},{8,16},{16,24},{24,32},{32,40},{40,48},{48,56},{56,64},{64,7... | collective-permute-start | bytes 98312 | tf_op jit(solution)/shard_map/ppermute | solution.py:23
  53.7 12.0 %collective-permute-done.7 = bf16[1,16,8,128]{3,2,1,0:T(8,128)(2,1)S(1)} collective-permute-done((bf16[1,16,8,128]{3,2,1,0:T(8,128)(2,1)S(1)}, bf16[1,16,8,128]{3,2,1,0:T(8,128)(2,1)S(1)}, u32[]{:S(2)}, u32[]{:S(2)}) %collective-permute-start.7) | collective-permute-done | bytes 32800 | tf_op jit(solution)/shard_map/ppermute | solution.py:26
  74.9 6.9 %broadcast_in_dim.241 = f32[9,128,256]{2,1,0:T(8,128)S(1)} reshape(f32[3,3,16,8,16,16]{5,4,3,2,1,0:T(8,128)} %broadcast_in_dim.240) | data formatting | bytes 2359296 | tf_op jit(solution)/shard_map/jit(_where)/broadcast_in_dim | solution.py:44
  81.7 4.3 %broadcast_in_dim.247 = f32[3,3,16,8,16,16]{5,4,3,2,1,0:T(8,128)} broadcast(f32[3,3,16,16]{3,2,1,0:T(8,128)S(1)} %get-tuple-element.36), dimensions={0,1,2,4} | broadcast | bytes 1188864 | tf_op jit(solution)/shard_map/jit(_where)/broadcast_in_dim | solution.py:44
  86.1 6.9 %broadcast_in_dim.248 = f32[9,128,256]{2,1,0:T(8,128)S(1)} reshape(f32[3,3,16,8,16,16]{5,4,3,2,1,0:T(8,128)} %broadcast_in_dim.247) | data formatting | bytes 2359296 | tf_op jit(solution)/shard_map/jit(_where)/broadcast_in_dim | solution.py:44
  92.9 4.3 %broadcast_in_dim.253 = f32[3,3,16,8,16,16]{5,4,3,2,1,0:T(8,128)} broadcast(f32[3,3,16,16]{3,2,1,0:T(8,128)S(1)} %get-tuple-element.35), dimensions={0,1,2,4} | broadcast | bytes 1188864 | tf_op jit(solution)/shard_map/jit(_where)/broadcast_in_dim | solution.py:44
  97.3 7.8 %broadcast_in_dim.254 = f32[9,128,256]{2,1,0:T(8,128)} reshape(f32[3,3,16,8,16,16]{5,4,3,2,1,0:T(8,128)} %broadcast_in_dim.253) | data formatting | bytes 2359296 | tf_op jit(solution)/shard_map/jit(_where)/broadcast_in_dim | solution.py:44
  105.1 4.3 %broadcast_in_dim.259 = f32[3,3,16,8,16,16]{5,4,3,2,1,0:T(8,128)} broadcast(f32[3,3,16,16]{3,2,1,0:T(8,128)S(1)} %copy-done.6), dimensions={0,1,2,4} | broadcast | bytes 1188864 | tf_op jit(solution)/shard_map/jit(_where)/broadcast_in_dim | solution.py:44
  109.4 7.8 %broadcast_in_dim.260 = f32[9,128,256]{2,1,0:T(8,128)} reshape(f32[3,3,16,8,16,16]{5,4,3,2,1,0:T(8,128)} %broadcast_in_dim.259) | data formatting | bytes 2359296 | tf_op jit(solution)/shard_map/jit(_where)/broadcast_in_dim | solution.py:44
  121.6 7.8 %broadcast_in_dim.263 = f32[9,128,256]{2,1,0:T(8,128)} reshape(f32[3,3,16,8,16,16]{5,4,3,2,1,0:T(8,128)} %broadcast_in_dim.262) | data formatting | bytes 2359296 | tf_op jit(solution)/shard_map/jit(_where)/broadcast_in_dim | solution.py:44
  133.7 7.9 %broadcast_in_dim.266 = f32[9,128,256]{2,1,0:T(8,128)} reshape(f32[3,3,16,8,16,16]{5,4,3,2,1,0:T(8,128)} %broadcast_in_dim.265) | data formatting | bytes 2359296 | tf_op jit(solution)/shard_map/jit(_where)/broadcast_in_dim | solution.py:44
  185.9 10.1 %collective-permute-done.13 = bf16[64,1,4,64]{0,3,2,1:T(8,128)(2,1)S(1)} collective-permute-done((bf16[64,1,4,64]{0,3,2,1:T(8,128)(2,1)S(1)}, bf16[64,1,4,64]{0,3,2,1:T(8,128)(2,1)S(1)}, u32[]{:S(2)}, u32[]{:S(2)}) %collective-permute-start.13) | collective-permute-done | bytes 32800 | tf_op jit(solution)/shard_map/ppermute | solution.py:26
  210.4 11.9 %fusion.50 = f32[1,64,4,4,64]{1,0,4,3,2:T(1,128)S(1)} fusion(bf16[3,3,3,64,64]{4,3,2,1,0:T(8,128)(2,1)S(1)} %reshape.135, bf16[1,64,6,6,66]{1,4,3,2,0:T(8,128)(2,1)S(1)} %maximum_bitcast_fusion), kind=kOutput, calls=%fused_computation.54 | convolution fusion | flops 226492416 | bytes 787456 | tf_op jit(solution)/shard_map/conv_general_dilated | solution.py:95
  223.7 15.7 %all_to_all.24 = bf16[256,2,64]{0,1,2:T(2,128)(2,1)S(1)} all-to-all(bf16[256,2,64]{0,1,2:T(2,128)(2,1)S(1)} %copy.175), channel_id=1, replica_groups=mesh['gx'=32,'gy'=2,'gz'=4] {'gx'}, dimensions={2} | all-to-all | bytes 131072 | tf_op jit(solution)/shard_map/all_to_all | solution.py:198
  242.9 7.0 %all-to-all-start.1 = ((bf16[256,64,2]{0,2,1:T(2,128)(2,1)}), bf16[256,64,2]{0,2,1:T(2,128)(2,1)S(1)}, u32[]{:S(2)}, u32[]{:S(2)}) async-start(bf16[256,64,2]{0,2,1:T(2,128)(2,1)} %copy.184), calls=%async_computation.1 | async-start | bytes 131072 | tf_op jit(solution)/shard_map/all_to_all | solution.py:204
  250.4 8.6 %all-to-all-done.1 = bf16[256,64,2]{0,2,1:T(2,128)(2,1)S(1)} async-done(((bf16[256,64,2]{0,2,1:T(2,128)(2,1)}), bf16[256,64,2]{0,2,1:T(2,128)(2,1)S(1)}, u32[]{:S(2)}, u32[]{:S(2)}) %all-to-all-start.1) | async-done | bytes 65568 | tf_op jit(solution)/shard_map/all_to_all | solution.py:204
  259.9 5.3 %collective-permute-start.18 = (bf16[64,1,4,64]{0,3,2,1:T(8,128)(2,1)S(1)}, bf16[64,1,4,64]{0,3,2,1:T(8,128)(2,1)S(1)}, u32[]{:S(2)}, u32[]{:S(2)}) collective-permute-start(bf16[64,1,4,64]{0,3,2,1:T(8,128)(2,1)S(1)} %get-tuple-element.23), channel_id=1, source_target_pairs={{0,8},{8,16},{16,24},{24,32},{32,40},{40,48},{48,56},{56,64},{64,7... | collective-permute-start | bytes 98312 | tf_op jit(solution)/shard_map/ppermute | solution.py:23
  267.2 12.3 %collective-permute-done.19 = bf16[64,1,4,64]{0,3,2,1:T(8,128)(2,1)S(1)} collective-permute-done((bf16[64,1,4,64]{0,3,2,1:T(8,128)(2,1)S(1)}, bf16[64,1,4,64]{0,3,2,1:T(8,128)(2,1)S(1)}, u32[]{:S(2)}, u32[]{:S(2)}) %collective-permute-start.19) | collective-permute-done | bytes 32800 | tf_op jit(solution)/shard_map/ppermute | solution.py:26
  288.8 4.5 %collective-permute-done.23 = bf16[64,6,1,66]{0,3,2,1:T(8,128)(2,1)S(1)} collective-permute-done((bf16[64,6,1,66]{0,3,2,1:T(8,128)(2,1)S(1)}, bf16[64,6,1,66]{0,3,2,1:T(8,128)(2,1)S(1)}, u32[]{:S(2)}, u32[]{:S(2)}) %collective-permute-start.23) | collective-permute-done | bytes 50720 | tf_op jit(solution)/shard_map/ppermute | solution.py:26
  293.6 11.9 %fusion.52 = f32[1,64,4,4,64]{1,0,4,3,2:T(1,128)S(1)} fusion(bf16[3,3,3,64,64]{4,3,2,1,0:T(8,128)(2,1)S(1)} %reshape.144, bf16[1,64,6,6,66]{1,4,3,2,0:T(8,128)(2,1)S(1)} %maximum_bitcast_fusion.1), kind=kOutput, calls=%fused_computation.56 | convolution fusion | flops 226492416 | bytes 787456 | tf_op jit(solution)/shard_map/conv_general_dilated | solution.py:95
  305.9 4.4 %copy.191 = f32[4,2,16,4,2,64,2]{2,6,5,4,3,1,0:T(2,128)} copy(f32[4,2,16,4,2,64,2]{5,2,6,4,1,3,0:T(8,128)S(1)} %convolution_bitcast_fusion) | data formatting | bytes 1048576 | tf_op jit(solution)/shard_map/ixvs,ioabc->xaovbsc/transpose | solution.py:128
  319.1 10.0 %collective-permute-done.25 = bf16[1,16,8,128]{3,2,1,0:T(8,128)(2,1)S(1)} collective-permute-done((bf16[1,16,8,128]{3,2,1,0:T(8,128)(2,1)S(1)}, bf16[1,16,8,128]{3,2,1,0:T(8,128)(2,1)S(1)}, u32[]{:S(2)}, u32[]{:S(2)}) %collective-permute-start.25) | collective-permute-done | bytes 32800 | tf_op jit(solution)/shard_map/ppermute | solution.py:26
  348.4 5.0 %shard_map.147 = f32[4,8,8,128]{3,2,1,0:T(8,128)} custom-call(bf16[10,256,256]{2,1,0:T(8,128)(2,1)} %bitcast.177, bf16[9,128,256]{2,1,0:T(8,128)(2,1)} %get-tuple-element.37.refs_1_, bf16[32,128]{1,0:T(8,128)(2,1)} %convert_element_type.143.refs_2_), custom_call_target="tpu_custom_call" | custom-call | tf_op jit(solution)/shard_map/pallas_call | solution.py:91
  (212 shorter events, 156.9 us)
Async XLA Ops:
  0.8 20.3 %collective-permute-start = (bf16[1,4,8,128]{3,2,0,1:T(8,128)(2,1)S(1)}, bf16[1,4,8,128]{3,2,0,1:T(8,128)(2,1)S(1)}, u32[]{:S(2)}, u32[]{:S(2)}) collective-permute-start(bf16[1,4,8,128]{3,2,0,1:T(8,128)(2,1)S(1)} %get-tuple-element.41), channel_id=1, source_target_pairs={{0,8},{8,16},{16,24},{24,32},{32,40},{40,48},{48,56},{56,64},{64,7... | collective-permute-start | bytes 24584 | tf_op jit(solution)/shard_map/ppermute | solution.py:23
  9.4 13.7 %collective-permute-start.1 = (bf16[1,4,8,128]{3,2,0,1:T(8,128)(2,1)S(1)}, bf16[1,4,8,128]{3,2,0,1:T(8,128)(2,1)S(1)}, u32[]{:S(2)}, u32[]{:S(2)}) collective-permute-start(bf16[1,4,8,128]{3,2,0,1:T(8,128)(2,1)S(1)} %get-tuple-element.42), channel_id=1, source_target_pairs={{8,0},{16,8},{24,16},{32,24},{40,32},{48,40},{56,48},{64,56},{72,6... | collective-permute-start | bytes 24584 | tf_op jit(solution)/shard_map/ppermute | solution.py:26
  27.9 4.6 %collective-permute-start.4 = (bf16[10,4,1,130]{3,2,0,1:T(2,128)(2,1)S(1)}, bf16[10,4,1,130]{3,2,0,1:T(2,128)(2,1)S(1)}, u32[]{:S(2)}, u32[]{:S(2)}) collective-permute-start(bf16[10,4,1,130]{3,2,0,1:T(2,128)(2,1)S(1)} %get-tuple-element.29), channel_id=1, source_target_pairs={{0,1},{1,2},{2,3},{4,5},{5,6},{6,7},{8,9},{9,10},{10,11},{12,13},{... | collective-permute-start | bytes 31208 | tf_op jit(solution)/shard_map/ppermute | solution.py:23
  30.8 5.9 %collective-permute-start.5 = (bf16[10,4,1,130]{3,2,0,1:T(2,128)(2,1)S(1)}, bf16[10,4,1,130]{3,2,0,1:T(2,128)(2,1)S(1)}, u32[]{:S(2)}, u32[]{:S(2)}) collective-permute-start(bf16[10,4,1,130]{3,2,0,1:T(2,128)(2,1)S(1)} %get-tuple-element.30), channel_id=1, source_target_pairs={{1,0},{2,1},{3,2},{5,4},{6,5},{7,6},{9,8},{10,9},{11,10},{13,12},{... | collective-permute-start | bytes 31208 | tf_op jit(solution)/shard_map/ppermute | solution.py:26
  41.7 11.9 %collective-permute-start.6 = (bf16[1,16,8,128]{3,2,1,0:T(8,128)(2,1)S(1)}, bf16[1,16,8,128]{3,2,1,0:T(8,128)(2,1)S(1)}, u32[]{:S(2)}, u32[]{:S(2)}) collective-permute-start(bf16[1,16,8,128]{3,2,1,0:T(8,128)(2,1)S(1)} %get-tuple-element.27), channel_id=1, source_target_pairs={{0,8},{8,16},{16,24},{24,32},{32,40},{40,48},{48,56},{56,64},{64,7... | collective-permute-start | bytes 98312 | tf_op jit(solution)/shard_map/ppermute | solution.py:23
  51.7 13.9 %collective-permute-start.7 = (bf16[1,16,8,128]{3,2,1,0:T(8,128)(2,1)S(1)}, bf16[1,16,8,128]{3,2,1,0:T(8,128)(2,1)S(1)}, u32[]{:S(2)}, u32[]{:S(2)}) collective-permute-start(bf16[1,16,8,128]{3,2,1,0:T(8,128)(2,1)S(1)} %get-tuple-element.28), channel_id=1, source_target_pairs={{8,0},{16,8},{24,16},{32,24},{40,32},{48,40},{56,48},{64,56},{72,6... | collective-permute-start | bytes 98312 | tf_op jit(solution)/shard_map/ppermute | solution.py:26
  66.7 82.3 %collective-permute-start.8 = (bf16[10,16,8,1]{3,2,1,0:T(8,128)(2,1)}, bf16[10,16,8,1]{3,2,1,0:T(8,128)(2,1)S(1)}, u32[]{:S(2)}, u32[]{:S(2)}) collective-permute-start(bf16[10,16,8,1]{3,2,1,0:T(8,128)(2,1)} %get-tuple-element.19), channel_id=1, source_target_pairs={{0,4},{1,5},{2,6},{3,7},{8,12},{9,13},{10,14},{11,15},{16,20},{17,... | collective-permute-start | bytes 7688 | tf_op jit(solution)/shard_map/ppermute | solution.py:23
  68.0 81.0 %collective-permute-start.9 = (bf16[10,16,8,1]{3,2,1,0:T(8,128)(2,1)}, bf16[10,16,8,1]{3,2,1,0:T(8,128)(2,1)S(1)}, u32[]{:S(2)}, u32[]{:S(2)}) collective-permute-start(bf16[10,16,8,1]{3,2,1,0:T(8,128)(2,1)} %get-tuple-element.20), channel_id=1, source_target_pairs={{4,0},{5,1},{6,2},{7,3},{12,8},{13,9},{14,10},{15,11},{20,16},{21,... | collective-permute-start | bytes 7688 | tf_op jit(solution)/shard_map/ppermute | solution.py:26
  149.8 8.0 %collective-permute-start.10 = (bf16[10,16,1,130]{3,2,1,0:T(2,128)(2,1)S(1)}, bf16[10,16,1,130]{3,2,1,0:T(2,128)(2,1)S(1)}, u32[]{:S(2)}, u32[]{:S(2)}) collective-permute-start(bf16[10,16,1,130]{3,2,1,0:T(2,128)(2,1)S(1)} %get-tuple-element.7), channel_id=1, source_target_pairs={{0,1},{1,2},{2,3},{4,5},{5,6},{6,7},{8,9},{9,10},{10,11},{12,13},{... | collective-permute-start | bytes 124808 | tf_op jit(solution)/shard_map/ppermute | solution.py:23
  152.8 8.9 %collective-permute-start.11 = (bf16[10,16,1,130]{3,2,1,0:T(2,128)(2,1)S(1)}, bf16[10,16,1,130]{3,2,1,0:T(2,128)(2,1)S(1)}, u32[]{:S(2)}, u32[]{:S(2)}) collective-permute-start(bf16[10,16,1,130]{3,2,1,0:T(2,128)(2,1)S(1)} %get-tuple-element.8), channel_id=1, source_target_pairs={{1,0},{2,1},{3,2},{5,4},{6,5},{7,6},{9,8},{10,9},{11,10},{13,12},{... | collective-permute-start | bytes 124808 | tf_op jit(solution)/shard_map/ppermute | solution.py:26
  179.8 6.2 %collective-permute-start.12 = (bf16[64,1,4,64]{0,3,2,1:T(8,128)(2,1)S(1)}, bf16[64,1,4,64]{0,3,2,1:T(8,128)(2,1)S(1)}, u32[]{:S(2)}, u32[]{:S(2)}) collective-permute-start(bf16[64,1,4,64]{0,3,2,1:T(8,128)(2,1)S(1)} %get-tuple-element.25), channel_id=1, source_target_pairs={{0,8},{8,16},{16,24},{24,32},{32,40},{40,48},{48,56},{56,64},{64,7... | collective-permute-start | bytes 98312 | tf_op jit(solution)/shard_map/ppermute | solution.py:23
  181.7 14.3 %collective-permute-start.13 = (bf16[64,1,4,64]{0,3,2,1:T(8,128)(2,1)S(1)}, bf16[64,1,4,64]{0,3,2,1:T(8,128)(2,1)S(1)}, u32[]{:S(2)}, u32[]{:S(2)}) collective-permute-start(bf16[64,1,4,64]{0,3,2,1:T(8,128)(2,1)S(1)} %get-tuple-element.26), channel_id=1, source_target_pairs={{8,0},{16,8},{24,16},{32,24},{40,32},{48,40},{56,48},{64,56},{72,6... | collective-permute-start | bytes 98312 | tf_op jit(solution)/shard_map/ppermute | solution.py:26
  200.5 5.6 %collective-permute-start.16 = (bf16[64,6,1,66]{0,3,2,1:T(8,128)(2,1)S(1)}, bf16[64,6,1,66]{0,3,2,1:T(8,128)(2,1)S(1)}, u32[]{:S(2)}, u32[]{:S(2)}) collective-permute-start(bf16[64,6,1,66]{0,3,2,1:T(8,128)(2,1)S(1)} %get-tuple-element.11), channel_id=1, source_target_pairs={{0,1},{1,2},{2,3},{4,5},{5,6},{6,7},{8,9},{9,10},{10,11},{12,13},{... | collective-permute-start | bytes 152072 | tf_op jit(solution)/shard_map/ppermute | solution.py:23
  203.4 6.7 %collective-permute-start.17 = (bf16[64,6,1,66]{0,3,2,1:T(8,128)(2,1)S(1)}, bf16[64,6,1,66]{0,3,2,1:T(8,128)(2,1)S(1)}, u32[]{:S(2)}, u32[]{:S(2)}) collective-permute-start(bf16[64,6,1,66]{0,3,2,1:T(8,128)(2,1)S(1)} %get-tuple-element.12), channel_id=1, source_target_pairs={{1,0},{2,1},{3,2},{5,4},{6,5},{7,6},{9,8},{10,9},{11,10},{13,12},{... | collective-permute-start | bytes 152072 | tf_op jit(solution)/shard_map/ppermute | solution.py:26
  242.9 16.1 %all-to-all-start.1 = ((bf16[256,64,2]{0,2,1:T(2,128)(2,1)}), bf16[256,64,2]{0,2,1:T(2,128)(2,1)S(1)}, u32[]{:S(2)}, u32[]{:S(2)}) async-start(bf16[256,64,2]{0,2,1:T(2,128)(2,1)} %copy.184), calls=%async_computation.1 | async-start | bytes 131072 | tf_op jit(solution)/shard_map/all_to_all | solution.py:204
  259.9 7.2 %collective-permute-start.18 = (bf16[64,1,4,64]{0,3,2,1:T(8,128)(2,1)S(1)}, bf16[64,1,4,64]{0,3,2,1:T(8,128)(2,1)S(1)}, u32[]{:S(2)}, u32[]{:S(2)}) collective-permute-start(bf16[64,1,4,64]{0,3,2,1:T(8,128)(2,1)S(1)} %get-tuple-element.23), channel_id=1, source_target_pairs={{0,8},{8,16},{16,24},{24,32},{32,40},{40,48},{48,56},{56,64},{64,7... | collective-permute-start | bytes 98312 | tf_op jit(solution)/shard_map/ppermute | solution.py:23
  265.2 14.3 %collective-permute-start.19 = (bf16[64,1,4,64]{0,3,2,1:T(8,128)(2,1)S(1)}, bf16[64,1,4,64]{0,3,2,1:T(8,128)(2,1)S(1)}, u32[]{:S(2)}, u32[]{:S(2)}) collective-permute-start(bf16[64,1,4,64]{0,3,2,1:T(8,128)(2,1)S(1)} %get-tuple-element.24), channel_id=1, source_target_pairs={{8,0},{16,8},{24,16},{32,24},{40,32},{48,40},{56,48},{64,56},{72,6... | collective-permute-start | bytes 98312 | tf_op jit(solution)/shard_map/ppermute | solution.py:26
  284.0 4.8 %collective-permute-start.22 = (bf16[64,6,1,66]{0,3,2,1:T(8,128)(2,1)S(1)}, bf16[64,6,1,66]{0,3,2,1:T(8,128)(2,1)S(1)}, u32[]{:S(2)}, u32[]{:S(2)}) collective-permute-start(bf16[64,6,1,66]{0,3,2,1:T(8,128)(2,1)S(1)} %get-tuple-element.9), channel_id=1, source_target_pairs={{0,1},{1,2},{2,3},{4,5},{5,6},{6,7},{8,9},{9,10},{10,11},{12,13},{... | collective-permute-start | bytes 152072 | tf_op jit(solution)/shard_map/ppermute | solution.py:23
  286.2 7.1 %collective-permute-start.23 = (bf16[64,6,1,66]{0,3,2,1:T(8,128)(2,1)S(1)}, bf16[64,6,1,66]{0,3,2,1:T(8,128)(2,1)S(1)}, u32[]{:S(2)}, u32[]{:S(2)}) collective-permute-start(bf16[64,6,1,66]{0,3,2,1:T(8,128)(2,1)S(1)} %get-tuple-element.10), channel_id=1, source_target_pairs={{1,0},{2,1},{3,2},{5,4},{6,5},{7,6},{9,8},{10,9},{11,10},{13,12},{... | collective-permute-start | bytes 152072 | tf_op jit(solution)/shard_map/ppermute | solution.py:26
  313.3 5.9 %collective-permute-start.24 = (bf16[1,16,8,128]{3,2,1,0:T(8,128)(2,1)S(1)}, bf16[1,16,8,128]{3,2,1,0:T(8,128)(2,1)S(1)}, u32[]{:S(2)}, u32[]{:S(2)}) collective-permute-start(bf16[1,16,8,128]{3,2,1,0:T(8,128)(2,1)S(1)} %get-tuple-element.21), channel_id=1, source_target_pairs={{0,8},{8,16},{16,24},{24,32},{32,40},{40,48},{48,56},{56,64},{64,7... | collective-permute-start | bytes 98312 | tf_op jit(solution)/shard_map/ppermute | solution.py:23
  315.2 13.9 %collective-permute-start.25 = (bf16[1,16,8,128]{3,2,1,0:T(8,128)(2,1)S(1)}, bf16[1,16,8,128]{3,2,1,0:T(8,128)(2,1)S(1)}, u32[]{:S(2)}, u32[]{:S(2)}) collective-permute-start(bf16[1,16,8,128]{3,2,1,0:T(8,128)(2,1)S(1)} %get-tuple-element.22), channel_id=1, source_target_pairs={{8,0},{16,8},{24,16},{32,24},{40,32},{48,40},{56,48},{64,56},{72,6... | collective-permute-start | bytes 98312 | tf_op jit(solution)/shard_map/ppermute | solution.py:26
  330.7 3.5 collective-permute-start.27
  335.0 6.1 %collective-permute-start.28 = (bf16[10,16,1,130]{3,2,1,0:T(2,128)(2,1)S(1)}, bf16[10,16,1,130]{3,2,1,0:T(2,128)(2,1)S(1)}, u32[]{:S(2)}, u32[]{:S(2)}) collective-permute-start(bf16[10,16,1,130]{3,2,1,0:T(2,128)(2,1)S(1)} %get-tuple-element.5), channel_id=1, source_target_pairs={{0,1},{1,2},{2,3},{4,5},{5,6},{6,7},{8,9},{9,10},{10,11},{12,13},{... | collective-permute-start | bytes 124808 | tf_op jit(solution)/shard_map/ppermute | solution.py:23
  337.4 7.9 %collective-permute-start.29 = (bf16[10,16,1,130]{3,2,1,0:T(2,128)(2,1)S(1)}, bf16[10,16,1,130]{3,2,1,0:T(2,128)(2,1)S(1)}, u32[]{:S(2)}, u32[]{:S(2)}) collective-permute-start(bf16[10,16,1,130]{3,2,1,0:T(2,128)(2,1)S(1)} %get-tuple-element.6), channel_id=1, source_target_pairs={{1,0},{2,1},{3,2},{5,4},{6,5},{7,6},{9,8},{10,9},{11,10},{13,12},{... | collective-permute-start | bytes 124808 | tf_op jit(solution)/shard_map/ppermute | solution.py:26
  (29 other events, 479.6 us)
